TPU v7x, 128 devices: a whole 4x4x4 slice. The times are simulated.
128 devices in a mesh: row: 8 (over x_hi, z), col: 16 (over x_lo, y, core).
Axes of the slice: x: 4 (x_hi: 2, x_lo: 2; x = x_hi * 2 + x_lo), y: 4, z: 4, core: 2. Of those that a mesh axis runs over, the one named last changes fastest.
Arguments:
- leaf_inverse: bfloat16 [2048, 256, 256], P(('row', 'col')), may hold values from -0.375 to 0.375
- leaf_coupling: bfloat16 [2048, 256, 256], P(('row', 'col')), may hold values from -0.375 to 0.375
- window_coupling: bfloat16 [2048, 256, 1024], P(('row', 'col')), may hold values from -6 to 6
- leaf_rows: int32 [2048, 256], P(('row', 'col')), may hold values from 0 to 2047
- leaf_sizes: int32 [2048], P(('row', 'col')), may hold values from 128 to 256
- owner_table: int32 [8, 32], P('row'), may hold values from 0 to 31, each once within a row
- schur_block: float32 [16384, 1024], P(('row', 'col')), may hold values from 0 to 1006
- prior_panels: float32 [16384, 1024], P(('row', 'col')), may hold values from -1 to 1
Outputs:
- result_panel: float32 [16384, 1024], P(('row', 'col'))
All inputs are finite; a program needn't handle non-finite values.
Results may differ from a plain program's by a relative error of at most 0.0003.
Values sent between devices are 32-bit elements; how exact they have to be, the bound alone decides.
No kernel may reach another device: no remote copies, remote signals or barrier semaphores. Data moves between devices by JAX's collectives and lax.ppermute only.
A program may use at most 128 MiB of HBM per device.

v0:
```python
import jax
import jax.numpy as jnp
from jax import lax
from jax.sharding import PartitionSpec as P

NB = 512
RB = 64


def blocked_factor(block, panel_width):
    symmetric = 0.5 * (block + block.T)
    panel_count = symmetric.shape[0] // panel_width
    factor = jnp.zeros_like(symmetric)
    trailing = symmetric
    for step_index in range(panel_count):
        leading = jnp.linalg.cholesky(trailing[:panel_width, :panel_width])
        beneath = jax.scipy.linalg.solve_triangular(
            leading, trailing[panel_width:, :panel_width].T, lower=True
        ).T
        offset = step_index * panel_width
        factor = factor.at[offset : offset + panel_width, offset : offset + panel_width].set(
            leading
        )
        factor = factor.at[offset + panel_width :, offset : offset + panel_width].set(beneath)
        trailing = trailing[panel_width:, panel_width:] - jnp.dot(
            beneath, beneath.T, precision=lax.Precision.HIGHEST
        )
    return factor


def body(
    leaf_inverse,
    leaf_coupling,
    window_coupling,
    leaf_rows,
    leaf_sizes,
    owner_table,
    schur_block,
    prior_panels,
):
    leaf_order = leaf_inverse.shape[1]
    col_width = window_coupling.shape[2]
    local_rows = schur_block.shape[0]
    group_rows = lax.axis_size("col") * local_rows
    window_rows = col_width // (lax.axis_size("row") * lax.axis_size("col"))
    position = jnp.arange(leaf_order, dtype=jnp.int32)
    active = position[None, :, None] < leaf_sizes[:, None, None]
    masked = jnp.where(active, window_coupling, jnp.zeros_like(window_coupling))
    solved = jnp.einsum("lij,ljw->liw", leaf_inverse, masked, preferred_element_type=jnp.float32)
    solved = jnp.where(active, solved, jnp.zeros_like(solved)).astype(jnp.bfloat16)
    leaf_terms = jnp.einsum(
        "lin,liw->lnw", leaf_coupling, solved, preferred_element_type=jnp.float32
    )
    summed = jnp.zeros((group_rows, col_width), jnp.float32)
    summed = summed.at[leaf_rows.reshape(-1)].add(leaf_terms.reshape(-1, col_width))
    blocks = summed.reshape(-1, RB, col_width)
    placed = jnp.zeros_like(blocks).at[owner_table[0]].set(blocks).reshape(group_rows, col_width)
    reduced = lax.psum_scatter(placed, "col", scatter_dimension=0, tiled=True)
    coupled = schur_block - reduced
    panels_win = lax.all_gather(prior_panels[:window_rows], ("row", "col"), axis=0, tiled=True)
    updated = coupled - jnp.dot(prior_panels, panels_win.T, precision=lax.Precision.HIGHEST)
    window_block = lax.all_gather(updated[:window_rows], ("row", "col"), axis=0, tiled=True)
    factor = blocked_factor(window_block, NB)
    return jax.scipy.linalg.solve_triangular(factor, updated.T, lower=True).T


def solution(mesh):
    placed = (
        P(("row", "col"), None, None),
        P(("row", "col"), None, None),
        P(("row", "col"), None, None),
        P(("row", "col"), None),
        P(("row", "col")),
        P("row", None),
        P(("row", "col"), None),
        P(("row", "col"), None),
    )
    return jax.shard_map(
        body, mesh=mesh, in_specs=placed, out_specs=P(("row", "col"), None), check_vma=False
    )
```

profile of v0, /device:TPU:1, one launch (start us, length us, event | category | flops | bytes accessed | tf_op | source)
XLA Modules:
  0.0 823.5 jit_solution(13366663568009760916)
XLA Ops:
  10.5 11.8 %fusion.8 = f32[16,1024,256]{1,2,0:T(8,128)} fusion(bf16[16,256,256]{2,1,0:T(8,128)(2,1)S(1)} %copy-done, bf16[16,256,256]{2,1,0:T(8,128)(2,1)} %param.15, bf16[16,256,1024]{2,1,0:T(8,128)(2,1)} %param.17, pred[16,256]{1,0:T(8,128)(4,1)S(1)} %iota_compare_fusion.4), kind=kOutput, calls=%fused_computation.16 | convolution fusion | flops 4307550208 | bytes 29364224 | tf_op jit(solution)/shard_map/lin,liw->lnw/dot_general | solution.py:51
  22.2 40.0 %scatter_custom_fusion = f32[2048,1024]{1,0:T(8,128)} fusion(s32[4096]{0:T(1024)S(1)} %bitcast.170, f32[4096,1024]{1,0:T(8,128)} %bitcast.171, f32[]{:T(128)} %constant.202.clone.1), kind=kCustom, calls=%fused_computation.12 | custom fusion | flops 4194304 | bytes 8389120 | tf_op jit(solution)/shard_map/scatter-add | solution.py:55
  66.5 15.4 %scatter_fusion = f32[32,64,1024]{2,1,0:T(8,128)} fusion(f32[32,64,1024]{2,1,0:T(8,128)} %broadcast_in_dim.36, s32[32]{0:T(128)S(1)} %fusion.81, f32[32,64,1024]{2,1,0:T(8,128)} %bitcast.158), kind=kCustom, calls=%fused_computation.1 | custom fusion | bytes 25165952 | tf_op jit(solution)/shard_map/scatter | solution.py:57
  82.2 136.0 %all-gather.3.cloned.1.call-done = f32[1024,1024]{1,0:T(8,128)} async-done(((f32[8,1024]{1,0:T(8,128)}), f32[1024,1024]{1,0:T(8,128)}) %all-gather.3.cloned.1.call-update) | async-done | bytes 4194320 | tf_op jit(solution)/shard_map/all_gather | solution.py:60
  218.2 6.7 convolution_subtract_fusion.1
  225.6 196.3 %all-gather.5.cloned.1.call-done = f32[1024,1024]{1,0:T(8,128)} async-done(((f32[8,1024]{1,0:T(8,128)}), f32[1024,1024]{1,0:T(8,128)}) %all-gather.5.cloned.1.call-update) | async-done | bytes 4194320 | tf_op jit(solution)/shard_map/all_gather | solution.py:62
  435.6 11.7 %cholesky.286 = f32[128,128]{1,0:T(8,128)S(1)} custom-call(f32[128,128]{1,0:T(8,128)S(1)} %cholesky.426), custom_call_target="Cholesky" | custom-call | tf_op jit(solution)/shard_map/jit(cholesky)/cholesky | solution.py:16
  447.4 9.8 %custom-call.33 = f32[1,128,128]{1,2,0:T(8,128)S(1)} custom-call(f32[1,128,128]{2,1,0:T(8,128)S(1)} %get-tuple-element.126), custom_call_target="InvertDiagBlocksLowerTriangular" | custom-call | tf_op jit(solution)/shard_map/jit(cholesky)/cholesky | solution.py:16
  457.9 12.1 %cholesky.305 = f32[128,128]{1,0:T(8,128)S(1)} custom-call(f32[128,128]{1,0:T(8,128)S(1)} %cholesky.430), custom_call_target="Cholesky" | custom-call | tf_op jit(solution)/shard_map/jit(cholesky)/cholesky | solution.py:16
  470.1 9.8 %custom-call.34 = f32[1,128,128]{1,2,0:T(8,128)S(1)} custom-call(f32[1,128,128]{2,1,0:T(8,128)S(1)} %get-tuple-element.123), custom_call_target="InvertDiagBlocksLowerTriangular" | custom-call | tf_op jit(solution)/shard_map/jit(cholesky)/cholesky | solution.py:16
  480.6 11.7 %cholesky.326 = f32[128,128]{1,0:T(8,128)S(1)} custom-call(f32[128,128]{1,0:T(8,128)S(1)} %cholesky.435), custom_call_target="Cholesky" | custom-call | tf_op jit(solution)/shard_map/jit(cholesky)/cholesky | solution.py:16
  493.0 9.8 %custom-call.35 = f32[1,128,128]{1,2,0:T(8,128)S(1)} custom-call(f32[1,128,128]{2,1,0:T(8,128)S(1)} %get-tuple-element.120), custom_call_target="InvertDiagBlocksLowerTriangular" | custom-call | tf_op jit(solution)/shard_map/jit(cholesky)/cholesky | solution.py:16
  503.4 11.9 %cholesky.343 = f32[128,128]{1,0:T(8,128)S(1)} custom-call(f32[128,128]{1,0:T(8,128)S(1)} %convolution_subtract_fusion.17), custom_call_target="Cholesky" | custom-call | tf_op jit(solution)/shard_map/jit(cholesky)/cholesky | solution.py:16
  520.3 14.3 %while.5 = (s32[]{:T(128)}, f32[512,512]{1,0:T(8,128)}, s32[4,2]{0,1:T(2,128)S(1)}, f32[4,128,128]{2,1,0:T(8,128)}, s32[]{:T(128)}) while((s32[]{:T(128)}, f32[512,512]{1,0:T(8,128)}, s32[4,2]{0,1:T(2,128)S(1)}, f32[4,128,128]{2,1,0:T(8,128)}, s32[]{:T(128)}) %tuple.85), condition=%wide.while_cond.3, body=%wide.while_body.3.sunk | while | flops 2 | bytes 132705 | solution.py:17
  534.6 40.1 %custom-call.28 = f32[4,128,128]{1,2,0:T(8,128)S(1)} custom-call(f32[4,128,128]{2,1,0:T(8,128)} %get-tuple-element.49), custom_call_target="InvertDiagBlocksLowerTriangular" | custom-call | tf_op jit(solution)/shard_map/jit(_solve_triangular)/triangular_solve | solution.py:17
  587.4 11.7 %cholesky.358 = f32[128,128]{1,0:T(8,128)S(1)} custom-call(f32[128,128]{1,0:T(8,128)S(1)} %cholesky.439), custom_call_target="Cholesky" | custom-call | tf_op jit(solution)/shard_map/jit(cholesky)/cholesky | solution.py:16
  599.3 9.8 %custom-call.36 = f32[1,128,128]{1,2,0:T(8,128)S(1)} custom-call(f32[1,128,128]{2,1,0:T(8,128)S(1)} %get-tuple-element.116), custom_call_target="InvertDiagBlocksLowerTriangular" | custom-call | tf_op jit(solution)/shard_map/jit(cholesky)/cholesky | solution.py:16
  612.6 11.7 %cholesky.377 = f32[128,128]{1,0:T(8,128)S(1)} custom-call(f32[128,128]{1,0:T(8,128)S(1)} %cholesky.443), custom_call_target="Cholesky" | custom-call | tf_op jit(solution)/shard_map/jit(cholesky)/cholesky | solution.py:16
  625.7 9.8 %custom-call.37 = f32[1,128,128]{1,2,0:T(8,128)S(1)} custom-call(f32[1,128,128]{2,1,0:T(8,128)S(1)} %get-tuple-element.113), custom_call_target="InvertDiagBlocksLowerTriangular" | custom-call | tf_op jit(solution)/shard_map/jit(cholesky)/cholesky | solution.py:16
  638.0 11.7 %cholesky.398 = f32[128,128]{1,0:T(8,128)S(1)} custom-call(f32[128,128]{1,0:T(8,128)S(1)} %cholesky.448), custom_call_target="Cholesky" | custom-call | tf_op jit(solution)/shard_map/jit(cholesky)/cholesky | solution.py:16
  650.5 10.2 %custom-call.38 = f32[1,128,128]{1,2,0:T(8,128)S(1)} custom-call(f32[1,128,128]{2,1,0:T(8,128)S(1)} %get-tuple-element.110), custom_call_target="InvertDiagBlocksLowerTriangular" | custom-call | tf_op jit(solution)/shard_map/jit(cholesky)/cholesky | solution.py:16
  662.1 11.7 %cholesky.415 = f32[128,128]{1,0:T(8,128)S(1)} custom-call(f32[128,128]{1,0:T(8,128)S(1)} %convolution_subtract_fusion.16), custom_call_target="Cholesky" | custom-call | tf_op jit(solution)/shard_map/jit(cholesky)/cholesky | solution.py:16
  686.5 28.1 %while.6 = (s32[]{:T(128)}, f32[1024,1024]{1,0:T(8,128)}, s32[8,2]{0,1:T(2,128)S(1)}, f32[8,128,128]{2,1,0:T(8,128)}, s32[]{:T(128)}) while((s32[]{:T(128)}, f32[1024,1024]{1,0:T(8,128)}, s32[8,2]{0,1:T(2,128)S(1)}, f32[8,128,128]{2,1,0:T(8,128)}, s32[]{:T(128)}) %tuple.88), condition=%wide.while_cond.4, body=%wide.while_body.4.sunk | while | flops 2 | bytes 132705 | solution.py:64
  714.6 80.2 %custom-call.29 = f32[8,128,128]{1,2,0:T(8,128)} custom-call(f32[8,128,128]{2,1,0:T(8,128)} %get-tuple-element.57), custom_call_target="InvertDiagBlocksLowerTriangular" | custom-call | tf_op jit(solution)/shard_map/jit(_solve_triangular)/triangular_solve | solution.py:64
  (164 shorter events, 123.1 us)
Async XLA Ops:
  7.4 3.1 copy-start
  7.4 210.8 %all-gather.3.cloned.1.call-start = ((), (), s32[]{:S(2)}) async-start(), calls=%async_computation.2 | async-start | bytes 4227072 | tf_op jit(solution)/shard_map/all_gather | solution.py:60
  8.9 209.2 %reduce-scatter.2.cloned.1.call-start = ((), (), s32[]{:S(2)}) async-start(), calls=%async_computation.1 | async-start | bytes 8912896 | tf_op jit(solution)/shard_map/reduce_scatter | solution.py:58
  22.2 40.0 %copy-start.16 = (s32[1,32]{1,0:T(1,128)S(1)}, s32[1,32]{1,0:T(1,128)}, u32[]{:S(2)}) copy-start(s32[1,32]{1,0:T(1,128)} %param.20) | copy-start | bytes 388
  81.9 136.2 %copy-start.13 = (f32[128,1024]{1,0:T(8,128)S(1)}, f32[128,1024]{1,0:T(8,128)}, u32[]{:S(2)}) copy-start(f32[128,1024]{1,0:T(8,128)} %param.22) | copy-start | bytes 1572868
  82.0 136.2 %copy-start.14 = (f32[128,1024]{1,0:T(8,128)S(1)}, f32[128,1024]{1,0:T(8,128)}, u32[]{:S(2)}) copy-start(f32[128,1024]{1,0:T(8,128)} %param.21) | copy-start | bytes 1572868
  82.0 339.9 %all-gather.5.cloned.1.call-start = ((), (), s32[]{:S(2)}) async-start(), calls=%async_computation.3 | async-start | bytes 4227072 | tf_op jit(solution)/shard_map/all_gather | solution.py:62
  224.8 202.4 %copy-start.10 = (f32[128,1024]{1,0:T(8,128)}, f32[128,1024]{1,0:T(8,128)S(1)}, u32[]{:S(2)}) copy-start(f32[128,1024]{1,0:T(8,128)S(1)} %convolution_subtract_fusion.1) | copy-start | bytes 1572868
  431.7 1.9 copy-start.2
  574.7 3.8 copy-start.15
  580.4 1.6 copy-start.4
  580.6 1.5 copy-start.6
  582.1 0.7 copy-start.8
  586.4 1.0 copy-start.3
  610.4 66.6 %copy-start.5 = (f32[128,512]{0,1:T(8,128)S(1)}, f32[128,512]{0,1:T(8,128)}, u32[]{:S(2)}) copy-start(f32[128,512]{0,1:T(8,128)} %copy-done.4) | copy-start | bytes 786436
  610.4 66.6 %copy-start.7 = (f32[128,512]{0,1:T(8,128)S(1)}, f32[128,512]{0,1:T(8,128)}, u32[]{:S(2)}) copy-start(f32[128,512]{0,1:T(8,128)} %copy-done.6) | copy-start | bytes 786436
  610.4 66.6 %copy-start.9 = (f32[128,512]{0,1:T(8,128)S(1)}, f32[128,512]{0,1:T(8,128)}, u32[]{:S(2)}) copy-start(f32[128,512]{0,1:T(8,128)} %copy-done.8) | copy-start | bytes 786436
  611.9 0.7 copy-start.12
  681.8 113.1 %copy-start.11 = (f32[128,1024]{1,0:T(8,128)S(1)}, f32[128,1024]{1,0:T(8,128)}, u32[]{:S(2)}) copy-start(f32[128,1024]{1,0:T(8,128)} %copy-done.10) | copy-start | bytes 1572868
  794.8 21.1 %copy-start.1 = (bf16[16,256,256]{2,1,0:T(8,128)(2,1)S(1)}, bf16[16,256,256]{2,1,0:T(8,128)(2,1)}, u32[]{:S(2)}) copy-start(bf16[16,256,256]{2,1,0:T(8,128)(2,1)} %param.16) | copy-start | bytes 6291460
Sparse Core Ops, SparseCore 0:
  9.9 208.2 all-gather.2
  225.6 196.1 all-gather.4
Sparse Core Ops, SparseCore 1:
  82.1 76.6 reduce-scatter.1
where the time goes:
time: 832 us; the launch traced here: 824 us
  other arithmetic  334 us (40%)
  waiting for transfers between devices  332 us (40%)
  local copies, waits for them, and re-layouts  79.7 us (10%)
  matrix products  56.8 us (7%)
  between operations  20.6 us (2%)
    all_gather x1, waiting for transfers between devices, body(): lax.all_gather(updated[:window_rows], ('row', 'col'), axis=0, tiled=True)  196 us
    another operation x29, other arithmetic, blocked_factor(): leading = jnp.linalg.cholesky(trailing[:panel_width, :panel_width])  158 us
    all_gather x1, waiting for transfers between devices, body(): lax.all_gather(prior_panels[:window_rows], ('row', 'col'), axis=0, tiled=...  136 us
    another operation x3, other arithmetic, body(): return jax.scipy.linalg.solve_triangular(factor, updated.T, lower=True).T  84.9 us
    another operation x36, local copies, waits for them, and re-layouts  42.4 us
    another operation x3, other arithmetic, blocked_factor(): jax.scipy.linalg.solve_triangular(leading, trailing[panel_width:, :panel_...  41.4 us
    scatter-add x1, other arithmetic, body(): summed.at[leaf_rows.reshape(-1)].add(leaf_terms.reshape(-1, col_width))  40 us
    another operation x15, matrix products, body(): return jax.scipy.linalg.solve_triangular(factor, updated.T, lower=True).T  20 us
  transfers between devices with their start and end apart: 3, of which 2 were waited for; matrix products, arithmetic and copies ran while one was open for 9% of the time, Pallas kernels for 0%

commit v1 on v0

--- a/solution.py
+++ b/solution.py
@@ -26,6 +26,11 @@
             beneath, beneath.T, precision=lax.Precision.HIGHEST
         )
     return factor
+
+
+def gather_rows(rows):
+    within = lax.all_gather(rows, "col", axis=0, tiled=True)
+    return lax.all_gather(within, "row", axis=0, tiled=True)
 
 
 def body(
@@ -57,9 +62,9 @@
     placed = jnp.zeros_like(blocks).at[owner_table[0]].set(blocks).reshape(group_rows, col_width)
     reduced = lax.psum_scatter(placed, "col", scatter_dimension=0, tiled=True)
     coupled = schur_block - reduced
-    panels_win = lax.all_gather(prior_panels[:window_rows], ("row", "col"), axis=0, tiled=True)
+    panels_win = gather_rows(prior_panels[:window_rows])
     updated = coupled - jnp.dot(prior_panels, panels_win.T, precision=lax.Precision.HIGHEST)
-    window_block = lax.all_gather(updated[:window_rows], ("row", "col"), axis=0, tiled=True)
+    window_block = gather_rows(updated[:window_rows])
     factor = blocked_factor(window_block, NB)
     return jax.scipy.linalg.solve_triangular(factor, updated.T, lower=True).T
 

time: 832 us -> 686 us (0.82)
  waiting for transfers between devices: 332 us -> 140 us
  blocking collectives: 0 us -> 47.4 us
    all_gather x2, waiting for transfers between devices: 332 us -> 69.7 us  [gather_rows(): return lax.all_gather(within, 'row', axis=0, tiled=True)]
    reduce_scatter x1, waiting for transfers between devices: 0.01 us -> 69.9 us  [body(): reduced = lax.psum_scatter(placed, 'col', scatter_dimension=0, tiled=True)]
    all_gather x0 -> x2, blocking collectives: none -> 47.4 us  [gather_rows(): within = lax.all_gather(rows, 'col', axis=0, tiled=True)]
  transfers between devices with their start and end apart: 3 -> 3, of which waited for: 2 -> 2; matrix products, arithmetic and copies ran while one was open for 9% -> 11% of each run, Pallas kernels for 0% -> 0%
where the time goes in v1:
time: 686 us; the launch traced here: 677 us
  other arithmetic  334 us (49%)
  waiting for transfers between devices  140 us (20%)
  local copies, waits for them, and re-layouts  78.3 us (11%)
  matrix products  56.8 us (8%)
  blocking collectives  47.4 us (7%)
  between operations  20.7 us (3%)
    another operation x29, other arithmetic, blocked_factor(): leading = jnp.linalg.cholesky(trailing[:panel_width, :panel_width])  158 us
    another operation x3, other arithmetic, body(): return jax.scipy.linalg.solve_triangular(factor, updated.T, lower=True).T  85 us
    reduce_scatter x1, waiting for transfers between devices, body(): reduced = lax.psum_scatter(placed, 'col', scatter_dimension=0, tiled=True)  69.9 us
    all_gather x2, waiting for transfers between devices, gather_rows(): return lax.all_gather(within, 'row', axis=0, tiled=True)  69.7 us
    all_gather x2, blocking collectives, gather_rows(): within = lax.all_gather(rows, 'col', axis=0, tiled=True)  47.4 us
    another operation x36, local copies, waits for them, and re-layouts  42.4 us
    another operation x3, other arithmetic, blocked_factor(): jax.scipy.linalg.solve_triangular(leading, trailing[panel_width:, :panel_...  41.4 us
    scatter-add x1, other arithmetic, body(): summed.at[leaf_rows.reshape(-1)].add(leaf_terms.reshape(-1, col_width))  40 us
  transfers between devices with their start and end apart: 3, of which 2 were waited for; matrix products, arithmetic and copies ran while one was open for 11% of the time, Pallas kernels for 0%

profile of v1, /device:TPU:1, one launch (start us, length us, event | category | flops | bytes accessed | tf_op | source)
XLA Modules:
  0.0 677.2 jit_solution(11012369915168135632)
XLA Ops:
  8.3 24.0 %all_gather.12 = f32[128,1024]{1,0:T(8,128)} all-gather(f32[8,1024]{1,0:T(8,128)S(1)} %slice.239), channel_id=1, replica_groups=mesh['row'=8,'col'=16] {'col'}, dimensions={0}, use_global_device_ids=true | all-gather | bytes 557056 | tf_op jit(solution)/shard_map/all_gather | solution.py:32
  33.9 11.8 %fusion.8 = f32[16,1024,256]{1,2,0:T(8,128)} fusion(bf16[16,256,256]{2,1,0:T(8,128)(2,1)S(1)} %copy-done, bf16[16,256,256]{2,1,0:T(8,128)(2,1)} %param.15, bf16[16,256,1024]{2,1,0:T(8,128)(2,1)} %param.17, pred[16,256]{1,0:T(8,128)(4,1)S(1)} %iota_compare_fusion.4), kind=kOutput, calls=%fused_computation.16 | convolution fusion | flops 4307550208 | bytes 29364224 | tf_op jit(solution)/shard_map/lin,liw->lnw/dot_general | solution.py:56
  45.6 40.0 %scatter_custom_fusion = f32[2048,1024]{1,0:T(8,128)} fusion(s32[4096]{0:T(1024)S(1)} %bitcast.170, f32[4096,1024]{1,0:T(8,128)} %bitcast.171, f32[]{:T(128)} %constant.202.clone.1), kind=kCustom, calls=%fused_computation.12 | custom fusion | flops 4194304 | bytes 8389120 | tf_op jit(solution)/shard_map/scatter-add | solution.py:60
  89.9 15.3 %scatter_fusion = f32[32,64,1024]{2,1,0:T(8,128)} fusion(f32[32,64,1024]{2,1,0:T(8,128)} %broadcast_in_dim.36, s32[32]{0:T(128)S(1)} %fusion.81, f32[32,64,1024]{2,1,0:T(8,128)} %bitcast.158), kind=kCustom, calls=%fused_computation.1 | custom fusion | bytes 25165952 | tf_op jit(solution)/shard_map/scatter | solution.py:62
  105.8 69.9 %reduce-scatter.2.cloned.1.call-done = f32[128,1024]{1,0:T(8,128)} async-done(((f32[2048,1024]{1,0:T(8,128)}), f32[128,1024]{1,0:T(8,128)}) %reduce-scatter.2.cloned.1.call-update) | async-done | bytes 524304 | tf_op jit(solution)/shard_map/reduce_scatter | solution.py:63
  182.4 23.4 %all_gather.14 = f32[128,1024]{1,0:T(8,128)} all-gather(f32[8,1024]{1,0:T(8,128)S(1)} %slice.266), channel_id=1, replica_groups=mesh['row'=8,'col'=16] {'col'}, dimensions={0}, use_global_device_ids=true | all-gather | bytes 557056 | tf_op jit(solution)/shard_map/all_gather | solution.py:32
  205.9 69.7 %all-gather.5.cloned.1.call-done = f32[1024,1024]{1,0:T(8,128)} async-done(((f32[128,1024]{1,0:T(8,128)}), f32[1024,1024]{1,0:T(8,128)}) %all-gather.5.cloned.1.call-update) | async-done | bytes 4194320 | tf_op jit(solution)/shard_map/all_gather | solution.py:33
  289.3 11.7 %cholesky.286 = f32[128,128]{1,0:T(8,128)S(1)} custom-call(f32[128,128]{1,0:T(8,128)S(1)} %cholesky.426), custom_call_target="Cholesky" | custom-call | tf_op jit(solution)/shard_map/jit(cholesky)/cholesky | solution.py:16
  301.2 9.8 %custom-call.33 = f32[1,128,128]{1,2,0:T(8,128)S(1)} custom-call(f32[1,128,128]{2,1,0:T(8,128)S(1)} %get-tuple-element.126), custom_call_target="InvertDiagBlocksLowerTriangular" | custom-call | tf_op jit(solution)/shard_map/jit(cholesky)/cholesky | solution.py:16
  311.7 11.9 %cholesky.305 = f32[128,128]{1,0:T(8,128)S(1)} custom-call(f32[128,128]{1,0:T(8,128)S(1)} %cholesky.430), custom_call_target="Cholesky" | custom-call | tf_op jit(solution)/shard_map/jit(cholesky)/cholesky | solution.py:16
  323.6 9.8 %custom-call.34 = f32[1,128,128]{1,2,0:T(8,128)S(1)} custom-call(f32[1,128,128]{2,1,0:T(8,128)S(1)} %get-tuple-element.123), custom_call_target="InvertDiagBlocksLowerTriangular" | custom-call | tf_op jit(solution)/shard_map/jit(cholesky)/cholesky | solution.py:16
  334.0 11.7 %cholesky.326 = f32[128,128]{1,0:T(8,128)S(1)} custom-call(f32[128,128]{1,0:T(8,128)S(1)} %cholesky.435), custom_call_target="Cholesky" | custom-call | tf_op jit(solution)/shard_map/jit(cholesky)/cholesky | solution.py:16
  346.5 9.8 %custom-call.35 = f32[1,128,128]{1,2,0:T(8,128)S(1)} custom-call(f32[1,128,128]{2,1,0:T(8,128)S(1)} %get-tuple-element.120), custom_call_target="InvertDiagBlocksLowerTriangular" | custom-call | tf_op jit(solution)/shard_map/jit(cholesky)/cholesky | solution.py:16
  356.9 12.1 %cholesky.343 = f32[128,128]{1,0:T(8,128)S(1)} custom-call(f32[128,128]{1,0:T(8,128)S(1)} %convolution_subtract_fusion.17), custom_call_target="Cholesky" | custom-call | tf_op jit(solution)/shard_map/jit(cholesky)/cholesky | solution.py:16
  374.1 14.3 %while.5 = (s32[]{:T(128)}, f32[512,512]{1,0:T(8,128)}, s32[4,2]{0,1:T(2,128)S(1)}, f32[4,128,128]{2,1,0:T(8,128)}, s32[]{:T(128)}) while((s32[]{:T(128)}, f32[512,512]{1,0:T(8,128)}, s32[4,2]{0,1:T(2,128)S(1)}, f32[4,128,128]{2,1,0:T(8,128)}, s32[]{:T(128)}) %tuple.85), condition=%wide.while_cond.3, body=%wide.while_body.3.sunk | while | flops 2 | bytes 132705 | solution.py:17
  388.3 40.1 %custom-call.28 = f32[4,128,128]{1,2,0:T(8,128)S(1)} custom-call(f32[4,128,128]{2,1,0:T(8,128)} %get-tuple-element.49), custom_call_target="InvertDiagBlocksLowerTriangular" | custom-call | tf_op jit(solution)/shard_map/jit(_solve_triangular)/triangular_solve | solution.py:17
  441.2 11.7 %cholesky.358 = f32[128,128]{1,0:T(8,128)S(1)} custom-call(f32[128,128]{1,0:T(8,128)S(1)} %cholesky.439), custom_call_target="Cholesky" | custom-call | tf_op jit(solution)/shard_map/jit(cholesky)/cholesky | solution.py:16
  453.0 9.8 %custom-call.36 = f32[1,128,128]{1,2,0:T(8,128)S(1)} custom-call(f32[1,128,128]{2,1,0:T(8,128)S(1)} %get-tuple-element.116), custom_call_target="InvertDiagBlocksLowerTriangular" | custom-call | tf_op jit(solution)/shard_map/jit(cholesky)/cholesky | solution.py:16
  466.3 11.7 %cholesky.377 = f32[128,128]{1,0:T(8,128)S(1)} custom-call(f32[128,128]{1,0:T(8,128)S(1)} %cholesky.443), custom_call_target="Cholesky" | custom-call | tf_op jit(solution)/shard_map/jit(cholesky)/cholesky | solution.py:16
  491.7 11.7 %cholesky.398 = f32[128,128]{1,0:T(8,128)S(1)} custom-call(f32[128,128]{1,0:T(8,128)S(1)} %cholesky.448), custom_call_target="Cholesky" | custom-call | tf_op jit(solution)/shard_map/jit(cholesky)/cholesky | solution.py:16
  504.2 10.0 %custom-call.38 = f32[1,128,128]{1,2,0:T(8,128)S(1)} custom-call(f32[1,128,128]{2,1,0:T(8,128)S(1)} %get-tuple-element.110), custom_call_target="InvertDiagBlocksLowerTriangular" | custom-call | tf_op jit(solution)/shard_map/jit(cholesky)/cholesky | solution.py:16
  515.6 11.7 %cholesky.415 = f32[128,128]{1,0:T(8,128)S(1)} custom-call(f32[128,128]{1,0:T(8,128)S(1)} %convolution_subtract_fusion.16), custom_call_target="Cholesky" | custom-call | tf_op jit(solution)/shard_map/jit(cholesky)/cholesky | solution.py:16
  540.0 28.1 %while.6 = (s32[]{:T(128)}, f32[1024,1024]{1,0:T(8,128)}, s32[8,2]{0,1:T(2,128)S(1)}, f32[8,128,128]{2,1,0:T(8,128)}, s32[]{:T(128)}) while((s32[]{:T(128)}, f32[1024,1024]{1,0:T(8,128)}, s32[8,2]{0,1:T(2,128)S(1)}, f32[8,128,128]{2,1,0:T(8,128)}, s32[]{:T(128)}) %tuple.88), condition=%wide.while_cond.4, body=%wide.while_body.4.sunk | while | flops 2 | bytes 132705 | solution.py:69
  568.1 80.3 %custom-call.29 = f32[8,128,128]{1,2,0:T(8,128)} custom-call(f32[8,128,128]{2,1,0:T(8,128)} %get-tuple-element.57), custom_call_target="InvertDiagBlocksLowerTriangular" | custom-call | tf_op jit(solution)/shard_map/jit(_solve_triangular)/triangular_solve | solution.py:69
  (166 shorter events, 138.5 us)
Async XLA Ops:
  7.4 26.5 %copy-start = (bf16[16,256,256]{2,1,0:T(8,128)(2,1)S(1)}, bf16[16,256,256]{2,1,0:T(8,128)(2,1)}, u32[]{:S(2)}) copy-start(bf16[16,256,256]{2,1,0:T(8,128)(2,1)} %param.16) | copy-start | bytes 6291460
  7.4 98.4 %all-gather.3.cloned.1.call-start = ((), (), s32[]{:S(2)}) async-start(), calls=%async_computation.2 | async-start | bytes 4718592 | tf_op jit(solution)/shard_map/all_gather | solution.py:33
  32.3 143.4 %reduce-scatter.2.cloned.1.call-start = ((), (), s32[]{:S(2)}) async-start(), calls=%async_computation.1 | async-start | bytes 8912896 | tf_op jit(solution)/shard_map/reduce_scatter | solution.py:63
  45.6 40.0 %copy-start.16 = (s32[1,32]{1,0:T(1,128)S(1)}, s32[1,32]{1,0:T(1,128)}, u32[]{:S(2)}) copy-start(s32[1,32]{1,0:T(1,128)} %param.20) | copy-start | bytes 388
  105.2 70.4 %copy-start.13 = (f32[128,1024]{1,0:T(8,128)S(1)}, f32[128,1024]{1,0:T(8,128)}, u32[]{:S(2)}) copy-start(f32[128,1024]{1,0:T(8,128)} %param.22) | copy-start | bytes 1572868
  105.2 70.4 %copy-start.14 = (f32[128,1024]{1,0:T(8,128)S(1)}, f32[128,1024]{1,0:T(8,128)}, u32[]{:S(2)}) copy-start(f32[128,1024]{1,0:T(8,128)} %param.21) | copy-start | bytes 1572868
  105.3 170.3 %all-gather.5.cloned.1.call-start = ((), (), s32[]{:S(2)}) async-start(), calls=%async_computation.3 | async-start | bytes 4718592 | tf_op jit(solution)/shard_map/all_gather | solution.py:33
  182.4 98.6 %copy-start.10 = (f32[128,1024]{1,0:T(8,128)}, f32[128,1024]{1,0:T(8,128)S(1)}, u32[]{:S(2)}) copy-start(f32[128,1024]{1,0:T(8,128)S(1)} %convolution_subtract_fusion.1) | copy-start | bytes 1572868
  285.4 1.9 copy-start.2
  428.5 3.8 copy-start.15
  434.1 1.6 copy-start.4
  434.3 1.5 copy-start.6
  435.8 0.7 copy-start.8
  440.2 1.0 copy-start.3
  464.1 66.4 %copy-start.5 = (f32[128,512]{0,1:T(8,128)S(1)}, f32[128,512]{0,1:T(8,128)}, u32[]{:S(2)}) copy-start(f32[128,512]{0,1:T(8,128)} %copy-done.4) | copy-start | bytes 786436
  464.1 66.4 %copy-start.7 = (f32[128,512]{0,1:T(8,128)S(1)}, f32[128,512]{0,1:T(8,128)}, u32[]{:S(2)}) copy-start(f32[128,512]{0,1:T(8,128)} %copy-done.6) | copy-start | bytes 786436
  464.1 66.4 %copy-start.9 = (f32[128,512]{0,1:T(8,128)S(1)}, f32[128,512]{0,1:T(8,128)}, u32[]{:S(2)}) copy-start(f32[128,512]{0,1:T(8,128)} %copy-done.8) | copy-start | bytes 786436
  465.6 0.7 copy-start.12
  535.3 113.1 %copy-start.11 = (f32[128,1024]{1,0:T(8,128)S(1)}, f32[128,1024]{1,0:T(8,128)}, u32[]{:S(2)}) copy-start(f32[128,1024]{1,0:T(8,128)} %copy-done.10) | copy-start | bytes 1572868
  648.4 21.1 %copy-start.1 = (bf16[16,256,256]{2,1,0:T(8,128)(2,1)S(1)}, bf16[16,256,256]{2,1,0:T(8,128)(2,1)}, u32[]{:S(2)}) copy-start(bf16[16,256,256]{2,1,0:T(8,128)(2,1)} %param.16) | copy-start | bytes 6291460
Sparse Core Ops, SparseCore 0:
  32.4 69.4 all-gather.2
  206.0 69.5 all-gather.4
Sparse Core Ops, SparseCore 1:
  105.4 70.3 reduce-scatter.1

commit v2 on v1

--- a/solution.py
+++ b/solution.py
@@ -1,31 +1,85 @@
 import jax
 import jax.numpy as jnp
 from jax import lax
+from jax.experimental import pallas as pl
+from jax.experimental.pallas import tpu as pltpu
 from jax.sharding import PartitionSpec as P
 
-NB = 512
 RB = 64
+BS = 128
+HI = lax.Precision.HIGHEST
 
 
-def blocked_factor(block, panel_width):
-    symmetric = 0.5 * (block + block.T)
-    panel_count = symmetric.shape[0] // panel_width
-    factor = jnp.zeros_like(symmetric)
-    trailing = symmetric
-    for step_index in range(panel_count):
-        leading = jnp.linalg.cholesky(trailing[:panel_width, :panel_width])
-        beneath = jax.scipy.linalg.solve_triangular(
-            leading, trailing[panel_width:, :panel_width].T, lower=True
-        ).T
-        offset = step_index * panel_width
-        factor = factor.at[offset : offset + panel_width, offset : offset + panel_width].set(
-            leading
-        )
-        factor = factor.at[offset + panel_width :, offset : offset + panel_width].set(beneath)
-        trailing = trailing[panel_width:, panel_width:] - jnp.dot(
-            beneath, beneath.T, precision=lax.Precision.HIGHEST
-        )
-    return factor
+def _nt(a, b):
+    return lax.dot_general(a, b, (((1,), (1,)), ((), ())), precision=HI,
+                           preferred_element_type=jnp.float32)
+
+
+def _nn(a, b):
+    return lax.dot_general(a, b, (((1,), (0,)), ((), ())), precision=HI,
+                           preferred_element_type=jnp.float32)
+
+
+def _block_inverse(blk_ref, inv_ref):
+    lane = lax.broadcasted_iota(jnp.int32, (1, BS), 1)
+    sub = lax.broadcasted_iota(jnp.int32, (BS, BS), 0)
+    inv_ref[...] = jnp.where(sub == lax.broadcasted_iota(jnp.int32, (BS, BS), 1), 1.0, 0.0).astype(jnp.float32)
+
+    def step(j, carry):
+        r = blk_ref[pl.ds(j, 1), :]
+        d = jnp.sum(jnp.where(lane == j, r, 0.0), axis=1, keepdims=True)
+        scale = 1.0 / jnp.sqrt(d)
+        c = jnp.where(lane >= j, r * scale, 0.0)
+        a = blk_ref[...]
+        col = jnp.sum(jnp.where(lax.broadcasted_iota(jnp.int32, (BS, BS), 1) == j, a, 0.0), axis=1, keepdims=True) * scale
+        col = jnp.where(lax.broadcasted_iota(jnp.int32, (BS, 1), 0) >= j, col, 0.0)
+        blk_ref[...] = a - col * c
+        m_row = inv_ref[pl.ds(j, 1), :] * scale
+        below = jnp.where(lax.broadcasted_iota(jnp.int32, (BS, 1), 0) > j, col, 0.0)
+        inv_ref[...] = inv_ref[...] - below * m_row
+        inv_ref[pl.ds(j, 1), :] = m_row
+        return carry
+
+    lax.fori_loop(0, BS, step, 0)
+
+
+def _kernel(s_ref, u_ref, o_ref, a_ref, l_ref, m_ref, blk_ref, inv_ref):
+    n = s_ref.shape[0]
+    nb = n // BS
+    a_ref[...] = s_ref[...]
+    for k in range(nb):
+        lo = k * BS
+        blk_ref[...] = a_ref[lo:lo + BS, lo:lo + BS]
+        _block_inverse(blk_ref, inv_ref)
+        mkk = inv_ref[...]
+        m_ref[k] = mkk
+        if k + 1 < nb:
+            panel = _nt(a_ref[lo + BS:, lo:lo + BS], mkk)
+            l_ref[lo + BS:, lo:lo + BS] = panel
+            a_ref[lo + BS:, lo + BS:] = a_ref[lo + BS:, lo + BS:] - _nt(panel, panel)
+    for j in range(nb):
+        lo = j * BS
+        acc = u_ref[:, lo:lo + BS]
+        if j > 0:
+            acc = acc - _nt(o_ref[:, :lo], l_ref[lo:lo + BS, :lo])
+        o_ref[:, lo:lo + BS] = _nt(acc, m_ref[j])
+
+
+def factor_solve(symmetric, rows):
+    n = symmetric.shape[0]
+    m = rows.shape[0]
+    return pl.pallas_call(
+        _kernel,
+        out_shape=jax.ShapeDtypeStruct((m, n), jnp.float32),
+        scratch_shapes=[
+            pltpu.VMEM((n, n), jnp.float32),
+            pltpu.VMEM((n, n), jnp.float32),
+            pltpu.VMEM((n // BS, BS, BS), jnp.float32),
+            pltpu.VMEM((BS, BS), jnp.float32),
+            pltpu.VMEM((BS, BS), jnp.float32),
+        ],
+        compiler_params=pltpu.CompilerParams(vmem_limit_bytes=60 * 1024 * 1024),
+    )(symmetric, rows)
 
 
 def gather_rows(rows):
@@ -65,8 +119,8 @@
     panels_win = gather_rows(prior_panels[:window_rows])
     updated = coupled - jnp.dot(prior_panels, panels_win.T, precision=lax.Precision.HIGHEST)
     window_block = gather_rows(updated[:window_rows])
-    factor = blocked_factor(window_block, NB)
-    return jax.scipy.linalg.solve_triangular(factor, updated.T, lower=True).T
+    symmetric = 0.5 * (window_block + window_block.T)
+    return factor_solve(symmetric, updated)
 
 
 def solution(mesh):

time: 686 us -> 438 us (0.64); the launches traced: 677 us -> 438 us
  other arithmetic: 334 us -> 47.6 us
  Pallas kernels: 0 us -> 143 us
  local copies, waits for them, and re-layouts: 78.3 us -> 26.7 us
  matrix products: 56.8 us -> 18.6 us
    another operation x35 -> x0, other arithmetic: 285 us -> none  [the longest x29 158 us: blocked_factor(): leading = jnp.linalg.cholesky(trailing[:panel_width, :panel_width])]
    pallas_call x0 -> x1, Pallas kernels: none -> 143 us  [factor_solve(): pl.pallas_call(_kernel, out_shape=jax.ShapeDtypeStruct((m, n), jnp.float3...]
    another operation x49 -> x0, local copies, waits for them, and re-layouts: 43 us -> none
    another operation x34 -> x0, matrix products: 35.3 us -> none  [the longest x15 20 us: body(): return jax.scipy.linalg.solve_triangular(factor, updated.T, lower=True).T]
  transfers between devices with their start and end apart: 3 -> 3, of which waited for: 2 -> 2; matrix products, arithmetic and copies ran while one was open for 11% -> 17% of each run, Pallas kernels for 0% -> 0%
where the time goes in v2:
time: 438 us
  Pallas kernels  143 us (33%)
  waiting for transfers between devices  140 us (32%)
  other arithmetic  47.6 us (11%)
  blocking collectives  47.4 us (11%)
  local copies, waits for them, and re-layouts  26.7 us (6%)
  matrix products  18.6 us (4%)
  between operations  14.9 us (3%)
    pallas_call x1, Pallas kernels, factor_solve(): pl.pallas_call(_kernel, out_shape=jax.ShapeDtypeStruct((m, n), jnp.float3...  143 us
    reduce_scatter x1, waiting for transfers between devices, body(): reduced = lax.psum_scatter(placed, 'col', scatter_dimension=0, tiled=True)  69.9 us
    all_gather x2, waiting for transfers between devices, gather_rows(): return lax.all_gather(within, 'row', axis=0, tiled=True)  69.6 us
    all_gather x2, blocking collectives, gather_rows(): within = lax.all_gather(rows, 'col', axis=0, tiled=True)  47.4 us
    scatter-add x1, other arithmetic, body(): summed.at[leaf_rows.reshape(-1)].add(leaf_terms.reshape(-1, col_width))  40 us
    scatter x1, local copies, waits for them, and re-layouts, body(): jnp.zeros_like(blocks).at[owner_table[0]].set(blocks)  15.3 us
    dot_general x1, matrix products, body(): jnp.einsum('lin,liw->lnw', leaf_coupling, solved, preferred_element_type=...  11.8 us
  transfers between devices with their start and end apart: 3, of which 2 were waited for; matrix products, arithmetic and copies ran while one was open for 17% of the time, Pallas kernels for 0%

profile of v2, /device:TPU:1, one launch (start us, length us, event | category | flops | bytes accessed | tf_op | source)
XLA Modules:
  0.0 437.6 jit_solution(17391205539061981484)
XLA Ops:
  7.4 0.0 copy-start
  7.4 0.9 slice.6
  8.3 24.0 %all_gather.12 = f32[128,1024]{1,0:T(8,128)} all-gather(f32[8,1024]{1,0:T(8,128)S(1)} %slice.6), channel_id=1, replica_groups=mesh['row'=8,'col'=16] {'col'}, dimensions={0}, use_global_device_ids=true | all-gather | bytes 557056 | tf_op jit(solution)/shard_map/all_gather | solution.py:86
  32.3 0.0 all-gather.3.cloned.1.call-update
  32.3 0.0 reduce-scatter.2.cloned.1.call-start
  32.4 0.7 copy.12
  33.1 0.7 iota_compare_fusion
  33.9 0.0 copy-done
  33.9 11.8 %fusion.7 = f32[16,1024,256]{1,2,0:T(8,128)} fusion(bf16[16,256,256]{2,1,0:T(8,128)(2,1)S(1)} %copy-done, bf16[16,256,256]{2,1,0:T(8,128)(2,1)} %param.8, bf16[16,256,1024]{2,1,0:T(8,128)(2,1)} %param.10, pred[16,256]{1,0:T(8,128)(4,1)S(1)} %iota_compare_fusion), kind=kOutput, calls=%fused_computation.10 | convolution fusion | flops 4307550208 | bytes 29364224 | tf_op jit(solution)/shard_map/lin,liw->lnw/dot_general | solution.py:110
  45.6 40.0 %scatter_custom_fusion = f32[2048,1024]{1,0:T(8,128)} fusion(s32[4096]{0:T(1024)S(1)} %bitcast.26, f32[4096,1024]{1,0:T(8,128)} %bitcast.27, f32[]{:T(128)} %constant.6.clone.1), kind=kCustom, calls=%fused_computation.8 | custom fusion | flops 4194304 | bytes 8389120 | tf_op jit(solution)/shard_map/scatter-add | solution.py:114
  85.6 4.3 broadcast_in_dim.32
  89.9 15.3 %scatter_fusion = f32[32,64,1024]{2,1,0:T(8,128)} fusion(f32[32,64,1024]{2,1,0:T(8,128)} %broadcast_in_dim.32, s32[32]{0:T(128)S(1)} %fusion.9, f32[32,64,1024]{2,1,0:T(8,128)} %bitcast.23), kind=kCustom, calls=%fused_computation.1 | custom fusion | bytes 25165952 | tf_op jit(solution)/shard_map/scatter | solution.py:116
  105.3 0.0 reduce-scatter.2.cloned.1.call-update
  105.3 0.2 all-gather.5.cloned.1.call-start
  105.5 0.0 all-gather.3.cloned.1.call-done
  105.6 69.9 %reduce-scatter.2.cloned.1.call-done = f32[128,1024]{1,0:T(8,128)} async-done(((f32[2048,1024]{1,0:T(8,128)}), f32[128,1024]{1,0:T(8,128)}) %reduce-scatter.2.cloned.1.call-update) | async-done | bytes 524304 | tf_op jit(solution)/shard_map/reduce_scatter | solution.py:117
  175.5 6.8 %convolution_subtract_fusion.u_ref = f32[128,1024]{1,0:T(8,128)S(1)} fusion(f32[128,1024]{1,0:T(8,128)S(1)} %copy-done.2, f32[1024,1024]{1,0:T(8,128)} %all-gather.3.cloned.1.call-done, f32[128,1024]{1,0:T(8,128)} %param.14, f32[128,1024]{1,0:T(8,128)} %reduce-scatter.2.cloned.1.call-done), kind=kOutput, calls=%fused_computation.11 | convolution fusion | flops 1610874880 | bytes 6291456 | tf_op jit(solution)/shard_map/dot_general | solution.py:120
  182.3 0.0 copy-start.1
  182.3 23.4 %all_gather.14 = f32[128,1024]{1,0:T(8,128)} all-gather(f32[8,1024]{1,0:T(8,128)S(1)} %slice.8), channel_id=1, replica_groups=mesh['row'=8,'col'=16] {'col'}, dimensions={0}, use_global_device_ids=true | all-gather | bytes 557056 | tf_op jit(solution)/shard_map/all_gather | solution.py:86
  205.7 0.0 all-gather.5.cloned.1.call-update
  205.8 69.6 %all-gather.5.cloned.1.call-done = f32[1024,1024]{1,0:T(8,128)} async-done(((f32[128,1024]{1,0:T(8,128)}), f32[1024,1024]{1,0:T(8,128)}) %all-gather.5.cloned.1.call-update) | async-done | bytes 4194320 | tf_op jit(solution)/shard_map/all_gather | solution.py:87
  275.4 5.4 %copy.10 = f32[1024,1024]{0,1:T(8,128)} copy(f32[1024,1024]{1,0:T(8,128)} %all-gather.5.cloned.1.call-done) | data formatting | bytes 8388608 | tf_op jit(solution)/shard_map/all_gather | solution.py:87
  280.7 6.9 %fusion.2.s_ref = f32[1024,1024]{1,0:T(8,128)} fusion(f32[1024,1024]{1,0:T(8,128)} %all-gather.5.cloned.1.call-done, f32[1024,1024]{0,1:T(8,128)} %copy.10), kind=kLoop, calls=%fused_computation.6 | loop fusion | flops 2097152 | bytes 12582912 | tf_op jit(solution)/shard_map/mul | solution.py:122
  287.6 142.6 %shard_map.82 = f32[128,1024]{1,0:T(8,128)} custom-call(f32[1024,1024]{1,0:T(8,128)} %fusion.2.s_ref, f32[128,1024]{1,0:T(8,128)} %copy-done.1), custom_call_target="tpu_custom_call" | custom-call | tf_op jit(solution)/shard_map/pallas_call | solution.py:71
  (9 shorter events, 0.0 us)
Async XLA Ops:
  7.4 26.5 %copy-start = (bf16[16,256,256]{2,1,0:T(8,128)(2,1)S(1)}, bf16[16,256,256]{2,1,0:T(8,128)(2,1)}, u32[]{:S(2)}) copy-start(bf16[16,256,256]{2,1,0:T(8,128)(2,1)} %param.9) | copy-start | bytes 6291460
  7.4 98.2 %all-gather.3.cloned.1.call-start = ((), (), s32[]{:S(2)}) async-start(), calls=%async_computation.2 | async-start | bytes 4718592 | tf_op jit(solution)/shard_map/all_gather | solution.py:87
  32.3 143.2 %reduce-scatter.2.cloned.1.call-start = ((), (), s32[]{:S(2)}) async-start(), calls=%async_computation.1 | async-start | bytes 8912896 | tf_op jit(solution)/shard_map/reduce_scatter | solution.py:117
  45.6 40.0 %copy-start.3 = (s32[1,32]{1,0:T(1,128)S(1)}, s32[1,32]{1,0:T(1,128)}, u32[]{:S(2)}) copy-start(s32[1,32]{1,0:T(1,128)} %param.13) | copy-start | bytes 388
  105.3 70.2 %copy-start.2 = (f32[128,1024]{1,0:T(8,128)S(1)}, f32[128,1024]{1,0:T(8,128)}, u32[]{:S(2)}) copy-start(f32[128,1024]{1,0:T(8,128)} %param.15) | copy-start | bytes 1572868
  105.3 170.1 %all-gather.5.cloned.1.call-start = ((), (), s32[]{:S(2)}) async-start(), calls=%async_computation.3 | async-start | bytes 4718592 | tf_op jit(solution)/shard_map/all_gather | solution.py:87
  182.3 105.3 %copy-start.1 = (f32[128,1024]{1,0:T(8,128)}, f32[128,1024]{1,0:T(8,128)S(1)}, u32[]{:S(2)}) copy-start(f32[128,1024]{1,0:T(8,128)S(1)} %convolution_subtract_fusion.u_ref) | copy-start | bytes 1572868
Sparse Core Ops, SparseCore 0:
  32.4 69.4 all-gather.2
  205.9 69.4 all-gather.4
Sparse Core Ops, SparseCore 1:
  105.4 70.0 reduce-scatter.1

commit v3 on v2

--- a/solution.py
+++ b/solution.py
@@ -83,8 +83,12 @@
 
 
 def gather_rows(rows):
-    within = lax.all_gather(rows, "col", axis=0, tiled=True)
-    return lax.all_gather(within, "row", axis=0, tiled=True)
+    n_row = lax.axis_size("row")
+    n_col = lax.axis_size("col")
+    across = lax.all_gather(rows, "row", axis=0, tiled=True)
+    both = lax.all_gather(across, "col", axis=0, tiled=True)
+    both = both.reshape(n_col, n_row, rows.shape[0], rows.shape[1])
+    return both.transpose(1, 0, 2, 3).reshape(-1, rows.shape[1])
 
 
 def body(
@@ -110,10 +114,9 @@
     leaf_terms = jnp.einsum(
         "lin,liw->lnw", leaf_coupling, solved, preferred_element_type=jnp.float32
     )
-    summed = jnp.zeros((group_rows, col_width), jnp.float32)
-    summed = summed.at[leaf_rows.reshape(-1)].add(leaf_terms.reshape(-1, col_width))
-    blocks = summed.reshape(-1, RB, col_width)
-    placed = jnp.zeros_like(blocks).at[owner_table[0]].set(blocks).reshape(group_rows, col_width)
+    targets = owner_table[0][leaf_rows // RB] * RB + leaf_rows % RB
+    placed = jnp.zeros((group_rows, col_width), jnp.float32)
+    placed = placed.at[targets.reshape(-1)].add(leaf_terms.reshape(-1, col_width))
     reduced = lax.psum_scatter(placed, "col", scatter_dimension=0, tiled=True)
     coupled = schur_block - reduced
     panels_win = gather_rows(prior_panels[:window_rows])

time: 438 us -> 445 us (1.016)
  waiting for transfers between devices: 140 us -> 119 us
  blocking collectives: 47.4 us -> 62.8 us
  local copies, waits for them, and re-layouts: 26.7 us -> 40.6 us
    gather x0 -> x1, local copies, waits for them, and re-layouts: none -> 24.7 us  [body(): targets = owner_table[0][leaf_rows // RB] * RB + leaf_rows % RB]
    all_gather x2, waiting for transfers between devices: 69.6 us -> 45.7 us  [gather_rows(): both = lax.all_gather(across, 'col', axis=0, tiled=True)]
    all_gather x2, blocking collectives: 47.4 us -> 62.8 us  [gather_rows(): across = lax.all_gather(rows, 'row', axis=0, tiled=True)]
    scatter x1 -> x0, local copies, waits for them, and re-layouts: 15.3 us -> none  [body(): jnp.zeros_like(blocks).at[owner_table[0]].set(blocks)]
    reshape x0 -> x2, local copies, waits for them, and re-layouts: none -> 10.1 us  [the longest x1 5.38 us: gather_rows(): return both.transpose(1, 0, 2, 3).reshape(-1, rows.shape[1])]
    all_gather x1 -> x0, local copies, waits for them, and re-layouts: 5.38 us -> none  [gather_rows(): return lax.all_gather(within, 'row', axis=0, tiled=True)]
    transpose x0 -> x1, local copies, waits for them, and re-layouts: none -> 4.78 us  [gather_rows(): return both.transpose(1, 0, 2, 3).reshape(-1, rows.shape[1])]
  transfers between devices with their start and end apart: 3 -> 3, of which waited for: 2 -> 2; matrix products, arithmetic and copies ran while one was open for 17% -> 18% of each run, Pallas kernels for 0% -> 0%
where the time goes in v3:
time: 445 us
  Pallas kernels  143 us (32%)
  waiting for transfers between devices  119 us (27%)
  blocking collectives  62.8 us (14%)
  other arithmetic  47.7 us (11%)
  local copies, waits for them, and re-layouts  40.6 us (9%)
  matrix products  18.7 us (4%)
  between operations  13.3 us (3%)
    pallas_call x1, Pallas kernels, factor_solve(): pl.pallas_call(_kernel, out_shape=jax.ShapeDtypeStruct((m, n), jnp.float3...  143 us
    reduce_scatter x1, waiting for transfers between devices, body(): reduced = lax.psum_scatter(placed, 'col', scatter_dimension=0, tiled=True)  73.5 us
    all_gather x2, blocking collectives, gather_rows(): across = lax.all_gather(rows, 'row', axis=0, tiled=True)  62.8 us
    all_gather x2, waiting for transfers between devices, gather_rows(): both = lax.all_gather(across, 'col', axis=0, tiled=True)  45.7 us
    scatter-add x1, other arithmetic, body(): placed.at[targets.reshape(-1)].add(leaf_terms.reshape(-1, col_width))  40 us
    gather x1, local copies, waits for them, and re-layouts, body(): targets = owner_table[0][leaf_rows // RB] * RB + leaf_rows % RB  24.7 us
    dot_general x1, matrix products, body(): jnp.einsum('lin,liw->lnw', leaf_coupling, solved, preferred_element_type=...  11.9 us
  transfers between devices with their start and end apart: 3, of which 2 were waited for; matrix products, arithmetic and copies ran while one was open for 18% of the time, Pallas kernels for 0%

profile of v3, /device:TPU:1, one launch (start us, length us, event | category | flops | bytes accessed | tf_op | source)
XLA Modules:
  0.0 445.1 jit_solution(4450231685515690838)
XLA Ops:
  6.5 0.9 slice.6
  7.5 32.2 %all_gather.12 = f32[64,1024]{1,0:T(8,128)} all-gather(f32[8,1024]{1,0:T(8,128)S(1)} %slice.6), channel_id=1, replica_groups=mesh['row'=8,'col'=16] {'row'}, dimensions={0}, use_global_device_ids=true | all-gather | bytes 294912 | tf_op jit(solution)/shard_map/all_gather | solution.py:88
  39.7 0.0 all-gather.3.cloned.1.call-update
  39.7 0.0 reduce-scatter.2.cloned.1.call-start
  39.8 0.7 fusion.11
  40.6 0.0 copy-start.4
  40.6 0.0 copy-start.5
  40.6 24.7 %gather_fusion = s32[4096]{0:T(1024)S(1)} fusion(s32[32]{0:T(128)S(1)} %bitcast.30, s32[4096]{0:T(1024)S(1)} %broadcast_clamp_fusion), kind=kCustom, calls=%fused_computation | custom fusion | bytes 49152 | tf_op jit(solution)/shard_map/gather | solution.py:117
  65.4 0.1 iota_compare_fusion
  65.5 11.9 %fusion.7 = f32[16,1024,256]{1,2,0:T(8,128)} fusion(bf16[16,256,256]{2,1,0:T(8,128)(2,1)S(1)} %copy-done, bf16[16,256,256]{2,1,0:T(8,128)(2,1)} %param.8, bf16[16,256,1024]{2,1,0:T(8,128)(2,1)} %param.10, pred[16,256]{1,0:T(8,128)(4,1)S(1)} %iota_compare_fusion), kind=kOutput, calls=%fused_computation.10 | convolution fusion | flops 4307550208 | bytes 29364224 | tf_op jit(solution)/shard_map/lin,liw->lnw/dot_general | solution.py:114
  77.4 40.0 %scatter_custom_fusion = f32[2048,1024]{1,0:T(8,128)} fusion(s32[4096]{0:T(1024)S(1)} %bitcast.37, f32[4096,1024]{1,0:T(8,128)} %bitcast.38, f32[]{:T(128)} %constant.31.clone.1), kind=kCustom, calls=%fused_computation.8 | custom fusion | flops 4194304 | bytes 8389120 | tf_op jit(solution)/shard_map/scatter-add | solution.py:119
  117.4 0.0 reduce-scatter.2.cloned.1.call-update
  117.4 0.2 all-gather.5.cloned.1.call-start
  117.6 0.0 all-gather.3.cloned.1.call-done
  117.7 4.8 %copy.17 = f32[8,16,8,1024]{3,2,1,0:T(8,128)} copy(f32[8,16,8,1024]{3,2,0,1:T(8,128)} %bitcast.33) | data formatting | bytes 8388608 | tf_op jit(solution)/shard_map/transpose | solution.py:91
  122.5 73.5 %reduce-scatter.2.cloned.1.call-done = f32[128,1024]{1,0:T(8,128)} async-done(((f32[2048,1024]{1,0:T(8,128)}), f32[128,1024]{1,0:T(8,128)}) %reduce-scatter.2.cloned.1.call-update) | async-done | bytes 524304 | tf_op jit(solution)/shard_map/reduce_scatter | solution.py:120
  196.0 6.8 %convolution_subtract_fusion.u_ref = f32[128,1024]{1,0:T(8,128)S(1)} fusion(f32[128,1024]{1,0:T(8,128)S(1)} %copy-done.3, f32[1024,1024]{1,0:T(8,128)} %bitcast.32, f32[128,1024]{1,0:T(8,128)} %param.14, f32[128,1024]{1,0:T(8,128)} %reduce-scatter.2.cloned.1.call-done), kind=kOutput, calls=%fused_computation.11 | convolution fusion | flops 1610874880 | bytes 6291456 | tf_op jit(solution)/shard_map/dot_general | solution.py:123
  202.8 30.5 %all_gather.14 = f32[64,1024]{1,0:T(8,128)} all-gather(f32[8,1024]{1,0:T(8,128)S(1)} %slice.10), channel_id=1, replica_groups=mesh['row'=8,'col'=16] {'row'}, dimensions={0}, use_global_device_ids=true | all-gather | bytes 294912 | tf_op jit(solution)/shard_map/all_gather | solution.py:88
  233.3 0.0 all-gather.5.cloned.1.call-update
  233.3 45.7 %all-gather.5.cloned.1.call-done = f32[1024,1024]{1,0:T(8,128)} async-done(((f32[64,1024]{1,0:T(8,128)}), f32[1024,1024]{1,0:T(8,128)}) %all-gather.5.cloned.1.call-update) | async-done | bytes 4194320 | tf_op jit(solution)/shard_map/all_gather | solution.py:89
  279.1 4.7 %copy.18 = f32[16,8,8,1024]{3,2,0,1:T(8,128)} copy(f32[16,8,8,1024]{3,2,1,0:T(8,128)} %bitcast.34) | data formatting | bytes 8388608 | tf_op jit(solution)/shard_map/reshape | solution.py:90
  283.8 5.4 %copy.19 = f32[1024,1024]{0,1:T(8,128)} copy(f32[1024,1024]{1,0:T(8,128)} %bitcast.31) | data formatting | bytes 8388608 | tf_op jit(solution)/shard_map/reshape | solution.py:91
  289.2 6.9 %fusion.2.s_ref = f32[1024,1024]{1,0:T(8,128)} fusion(f32[1024,1024]{0,1:T(8,128)} %copy.19, f32[16,8,8,1024]{3,2,0,1:T(8,128)} %copy.18), kind=kLoop, calls=%fused_computation.6 | loop fusion | flops 2097152 | bytes 12582912 | tf_op jit(solution)/shard_map/mul | solution.py:125
  296.0 142.6 %shard_map.82 = f32[128,1024]{1,0:T(8,128)} custom-call(f32[1024,1024]{1,0:T(8,128)} %fusion.2.s_ref, f32[128,1024]{1,0:T(8,128)} %copy-done.2), custom_call_target="tpu_custom_call" | custom-call | tf_op jit(solution)/shard_map/pallas_call | solution.py:71
  (19 shorter events, 0.1 us)
Async XLA Ops:
  6.5 58.9 %copy-start = (bf16[16,256,256]{2,1,0:T(8,128)(2,1)S(1)}, bf16[16,256,256]{2,1,0:T(8,128)(2,1)}, u32[]{:S(2)}) copy-start(bf16[16,256,256]{2,1,0:T(8,128)(2,1)} %param.9) | copy-start | bytes 6291460
  6.5 34.0 %copy-start.1 = (s32[1,32]{1,0:T(1,128)S(1)}, s32[1,32]{1,0:T(1,128)}, u32[]{:S(2)}) copy-start(s32[1,32]{1,0:T(1,128)} %param.13) | copy-start | bytes 388
  6.5 111.1 %all-gather.3.cloned.1.call-start = ((), (), s32[]{:S(2)}) async-start(), calls=%async_computation.2 | async-start | bytes 4456448 | tf_op jit(solution)/shard_map/all_gather | solution.py:89
  39.7 156.2 %reduce-scatter.2.cloned.1.call-start = ((), (), s32[]{:S(2)}) async-start(), calls=%async_computation.1 | async-start | bytes 8912896 | tf_op jit(solution)/shard_map/reduce_scatter | solution.py:120
  40.6 24.8 %copy-start.4 = (s32[16,256]{1,0:T(8,128)S(1)}, s32[16,256]{1,0:T(8,128)}, u32[]{:S(2)}) copy-start(s32[16,256]{1,0:T(8,128)} %param.11) | copy-start | bytes 49156
  40.6 24.8 %copy-start.5 = (s32[16]{0:T(128)S(1)}, s32[16]{0:T(128)}, u32[]{:S(2)}) copy-start(s32[16]{0:T(128)} %param.12) | copy-start | bytes 196
  117.4 161.6 %all-gather.5.cloned.1.call-start = ((), (), s32[]{:S(2)}) async-start(), calls=%async_computation.3 | async-start | bytes 4456448 | tf_op jit(solution)/shard_map/all_gather | solution.py:89
  117.7 78.3 %copy-start.3 = (f32[128,1024]{1,0:T(8,128)S(1)}, f32[128,1024]{1,0:T(8,128)}, u32[]{:S(2)}) copy-start(f32[128,1024]{1,0:T(8,128)} %param.15) | copy-start | bytes 1572868
  202.8 81.0 %copy-start.2 = (f32[128,1024]{1,0:T(8,128)}, f32[128,1024]{1,0:T(8,128)S(1)}, u32[]{:S(2)}) copy-start(f32[128,1024]{1,0:T(8,128)S(1)} %convolution_subtract_fusion.u_ref) | copy-start | bytes 1572868
Sparse Core Ops, SparseCore 0:
  39.8 44.9 all-gather.2
  117.5 78.3 reduce-scatter.1
  233.5 45.5 all-gather.4

commit v4 on v3

--- a/solution.py
+++ b/solution.py
@@ -82,6 +82,11 @@
     )(symmetric, rows)
 
 
+def gather_rows_col_first(rows):
+    within = lax.all_gather(rows, "col", axis=0, tiled=True)
+    return lax.all_gather(within, "row", axis=0, tiled=True)
+
+
 def gather_rows(rows):
     n_row = lax.axis_size("row")
     n_col = lax.axis_size("col")
@@ -114,13 +119,19 @@
     leaf_terms = jnp.einsum(
         "lin,liw->lnw", leaf_coupling, solved, preferred_element_type=jnp.float32
     )
-    targets = owner_table[0][leaf_rows // RB] * RB + leaf_rows % RB
+    block_of = leaf_rows // RB
+    slots = lax.broadcasted_iota(jnp.int32, (1, 1, owner_table.shape[1]), 2)
+    shift = jnp.sum(
+        jnp.where(block_of[:, :, None] == slots, owner_table[0][None, None, :] - slots, 0), axis=2
+    )
+    targets = leaf_rows + shift * RB
     placed = jnp.zeros((group_rows, col_width), jnp.float32)
     placed = placed.at[targets.reshape(-1)].add(leaf_terms.reshape(-1, col_width))
     reduced = lax.psum_scatter(placed, "col", scatter_dimension=0, tiled=True)
-    coupled = schur_block - reduced
-    panels_win = gather_rows(prior_panels[:window_rows])
-    updated = coupled - jnp.dot(prior_panels, panels_win.T, precision=lax.Precision.HIGHEST)
+    panels_win = gather_rows_col_first(prior_panels[:window_rows])
+    partial = schur_block - jnp.dot(prior_panels, panels_win.T, precision=lax.Precision.HIGHEST)
+    partial = lax.optimization_barrier(partial)
+    updated = partial - reduced
     window_block = gather_rows(updated[:window_rows])
     symmetric = 0.5 * (window_block + window_block.T)
     return factor_solve(symmetric, updated)

time: 445 us -> 402 us (0.903)
  local copies, waits for them, and re-layouts: 40.6 us -> 11 us
  waiting for transfers between devices: 119 us -> 109 us
  blocking collectives: 62.8 us -> 54.5 us
    all_gather x2 -> x1, blocking collectives: 62.8 us -> 30.5 us  [gather_rows(): across = lax.all_gather(rows, 'row', axis=0, tiled=True)]
    reduce_scatter x1, waiting for transfers between devices: 73.5 us -> 48.6 us  [body(): reduced = lax.psum_scatter(placed, 'col', scatter_dimension=0, tiled=True)]
    gather x1 -> x0, local copies, waits for them, and re-layouts: 24.7 us -> none  [body(): targets = owner_table[0][leaf_rows // RB] * RB + leaf_rows % RB]
    all_gather x0 -> x1, blocking collectives: none -> 24 us  [gather_rows_col_first(): within = lax.all_gather(rows, 'col', axis=0, tiled=True)]
    all_gather x0 -> x1, waiting for transfers between devices: none -> 14.7 us  [gather_rows_col_first(): return lax.all_gather(within, 'row', axis=0, tiled=True)]
    transpose x1 -> x0, local copies, waits for them, and re-layouts: 4.78 us -> none  [gather_rows(): return both.transpose(1, 0, 2, 3).reshape(-1, rows.shape[1])]
    all_gather x2 -> x1, waiting for transfers between devices: 45.7 us -> 45.6 us  [gather_rows(): both = lax.all_gather(across, 'col', axis=0, tiled=True)]
  transfers between devices with their start and end apart: 3 -> 3, of which waited for: 2 -> 3; matrix products, arithmetic and copies ran while one was open for 18% -> 15% of each run, Pallas kernels for 0% -> 0%
where the time goes in v4:
time: 402 us
  Pallas kernels  143 us (36%)
  waiting for transfers between devices  109 us (27%)
  blocking collectives  54.5 us (14%)
  other arithmetic  51 us (13%)
  matrix products  18.5 us (5%)
  between operations  14.9 us (4%)
  local copies, waits for them, and re-layouts  11 us (3%)
    pallas_call x1, Pallas kernels, factor_solve(): pl.pallas_call(_kernel, out_shape=jax.ShapeDtypeStruct((m, n), jnp.float3...  143 us
    reduce_scatter x1, waiting for transfers between devices, body(): reduced = lax.psum_scatter(placed, 'col', scatter_dimension=0, tiled=True)  48.6 us
    all_gather x1, waiting for transfers between devices, gather_rows(): both = lax.all_gather(across, 'col', axis=0, tiled=True)  45.6 us
    scatter-add x1, other arithmetic, body(): placed.at[targets.reshape(-1)].add(leaf_terms.reshape(-1, col_width))  40 us
    all_gather x1, blocking collectives, gather_rows(): across = lax.all_gather(rows, 'row', axis=0, tiled=True)  30.5 us
    all_gather x1, blocking collectives, gather_rows_col_first(): within = lax.all_gather(rows, 'col', axis=0, tiled=True)  24 us
    all_gather x1, waiting for transfers between devices, gather_rows_col_first(): return lax.all_gather(within, 'row', axis=0, tiled=True)  14.7 us
    dot_general x1, matrix products, body(): jnp.einsum('lin,liw->lnw', leaf_coupling, solved, preferred_element_type=...  11.8 us
  transfers between devices with their start and end apart: 3, of which 3 were waited for; matrix products, arithmetic and copies ran while one was open for 15% of the time, Pallas kernels for 0%

profile of v4, /device:TPU:1, one launch (start us, length us, event | category | flops | bytes accessed | tf_op | source)
XLA Modules:
  0.0 401.5 jit_solution(6210494895198297814)
XLA Ops:
  7.4 0.9 slice.6
  8.3 24.0 %all_gather.12 = f32[128,1024]{1,0:T(8,128)} all-gather(f32[8,1024]{1,0:T(8,128)S(1)} %slice.6), channel_id=1, replica_groups=mesh['row'=8,'col'=16] {'col'}, dimensions={0}, use_global_device_ids=true | all-gather | bytes 557056 | tf_op jit(solution)/shard_map/all_gather | solution.py:86
  32.3 0.0 all-gather.3.cloned.1.call-update
  32.3 0.0 reduce-scatter.2.cloned.1.call-start
  32.4 0.7 bitcast_subtract_fusion
  33.0 0.7 add_select_fusion
  33.7 0.2 select_reduce_fusion
  33.9 0.7 add_bitcast_fusion
  34.7 0.7 iota_compare_fusion.1
  35.4 11.8 %fusion.7 = f32[16,1024,256]{1,2,0:T(8,128)} fusion(bf16[16,256,256]{2,1,0:T(8,128)(2,1)S(1)} %copy-done, bf16[16,256,256]{2,1,0:T(8,128)(2,1)} %param.8, bf16[16,256,1024]{2,1,0:T(8,128)(2,1)} %param.10, pred[16,256]{1,0:T(8,128)(4,1)S(1)} %iota_compare_fusion.1), kind=kOutput, calls=%fused_computation.9 | convolution fusion | flops 4307550208 | bytes 29364224 | tf_op jit(solution)/shard_map/lin,liw->lnw/dot_general | solution.py:119
  47.2 40.0 %scatter_custom_fusion = f32[2048,1024]{1,0:T(8,128)} fusion(s32[4096]{0:T(1024)S(1)} %bitcast.27, f32[4096,1024]{1,0:T(8,128)} %bitcast.28, f32[]{:T(128)} %constant.10.clone.1), kind=kCustom, calls=%fused_computation.7 | custom fusion | flops 4194304 | bytes 8389120 | tf_op jit(solution)/shard_map/scatter-add | solution.py:129
  87.2 0.0 reduce-scatter.2.cloned.1.call-update
  87.2 0.0 all-gather.5.cloned.1.call-start
  87.3 14.7 %all-gather.3.cloned.1.call-done = f32[1024,1024]{1,0:T(8,128)} async-done(((f32[128,1024]{1,0:T(8,128)}), f32[1024,1024]{1,0:T(8,128)}) %all-gather.3.cloned.1.call-update) | async-done | bytes 4194320 | tf_op jit(solution)/shard_map/all_gather | solution.py:87
  101.9 6.8 %convolution_subtract_fusion = f32[128,1024]{1,0:T(8,128)S(1)} fusion(f32[128,1024]{1,0:T(8,128)} %param.14, f32[128,1024]{1,0:T(8,128)S(1)} %copy-done.2, f32[1024,1024]{1,0:T(8,128)} %all-gather.3.cloned.1.call-done), kind=kOutput, calls=%fused_computation.10 | convolution fusion | flops 1610743808 | bytes 5767168 | tf_op jit(solution)/shard_map/dot_general | solution.py:132
  108.7 48.6 %reduce-scatter.2.cloned.1.call-done = f32[128,1024]{1,0:T(8,128)} async-done(((f32[2048,1024]{1,0:T(8,128)}), f32[128,1024]{1,0:T(8,128)}) %reduce-scatter.2.cloned.1.call-update) | async-done | bytes 524304 | tf_op jit(solution)/shard_map/reduce_scatter | solution.py:130
  157.4 1.1 sub.23.u_ref
  158.5 30.5 %all_gather.14 = f32[64,1024]{1,0:T(8,128)} all-gather(f32[8,1024]{1,0:T(8,128)S(1)} %slice.8), channel_id=1, replica_groups=mesh['row'=8,'col'=16] {'row'}, dimensions={0}, use_global_device_ids=true | all-gather | bytes 294912 | tf_op jit(solution)/shard_map/all_gather | solution.py:93
  189.0 0.0 all-gather.5.cloned.1.call-update
  189.0 45.6 %all-gather.5.cloned.1.call-done = f32[1024,1024]{1,0:T(8,128)} async-done(((f32[64,1024]{1,0:T(8,128)}), f32[1024,1024]{1,0:T(8,128)}) %all-gather.5.cloned.1.call-update) | async-done | bytes 4194320 | tf_op jit(solution)/shard_map/all_gather | solution.py:94
  234.6 4.7 %copy.17 = f32[16,8,8,1024]{3,2,0,1:T(8,128)} copy(f32[16,8,8,1024]{3,2,1,0:T(8,128)} %bitcast.25) | data formatting | bytes 8388608 | tf_op jit(solution)/shard_map/reshape | solution.py:95
  239.3 5.4 %copy.18 = f32[1024,1024]{0,1:T(8,128)} copy(f32[1024,1024]{1,0:T(8,128)} %bitcast.24) | data formatting | bytes 8388608 | tf_op jit(solution)/shard_map/reshape | solution.py:96
  244.7 6.9 %fusion.2.s_ref = f32[1024,1024]{1,0:T(8,128)} fusion(f32[1024,1024]{0,1:T(8,128)} %copy.18, f32[16,8,8,1024]{3,2,0,1:T(8,128)} %copy.17), kind=kLoop, calls=%fused_computation.5 | loop fusion | flops 2097152 | bytes 12582912 | tf_op jit(solution)/shard_map/mul | solution.py:136
  251.6 142.6 %shard_map.82 = f32[128,1024]{1,0:T(8,128)} custom-call(f32[1024,1024]{1,0:T(8,128)} %fusion.2.s_ref, f32[128,1024]{1,0:T(8,128)} %copy-done.1), custom_call_target="tpu_custom_call" | custom-call | tf_op jit(solution)/shard_map/pallas_call | solution.py:71
  (10 shorter events, 0.1 us)
Async XLA Ops:
  7.4 28.1 %copy-start = (bf16[16,256,256]{2,1,0:T(8,128)(2,1)S(1)}, bf16[16,256,256]{2,1,0:T(8,128)(2,1)}, u32[]{:S(2)}) copy-start(bf16[16,256,256]{2,1,0:T(8,128)(2,1)} %param.9) | copy-start | bytes 6291460
  7.4 94.6 %all-gather.3.cloned.1.call-start = ((), (), s32[]{:S(2)}) async-start(), calls=%async_computation.1 | async-start | bytes 4718592 | tf_op jit(solution)/shard_map/all_gather | solution.py:87
  32.3 125.0 %reduce-scatter.2.cloned.1.call-start = ((), (), s32[]{:S(2)}) async-start(), calls=%async_computation.2 | async-start | bytes 8912896 | tf_op jit(solution)/shard_map/reduce_scatter | solution.py:130
  47.2 54.7 %copy-start.2 = (f32[128,1024]{1,0:T(8,128)S(1)}, f32[128,1024]{1,0:T(8,128)}, u32[]{:S(2)}) copy-start(f32[128,1024]{1,0:T(8,128)} %param.15) | copy-start | bytes 1572868
  87.2 147.4 %all-gather.5.cloned.1.call-start = ((), (), s32[]{:S(2)}) async-start(), calls=%async_computation.3 | async-start | bytes 4456448 | tf_op jit(solution)/shard_map/all_gather | solution.py:94
  158.5 86.2 %copy-start.1 = (f32[128,1024]{1,0:T(8,128)}, f32[128,1024]{1,0:T(8,128)S(1)}, u32[]{:S(2)}) copy-start(f32[128,1024]{1,0:T(8,128)S(1)} %sub.23.u_ref) | copy-start | bytes 1572868
Sparse Core Ops, SparseCore 0:
  32.4 69.4 all-gather.2
Sparse Core Ops, SparseCore 1:
  87.3 70.0 reduce-scatter.1
  189.1 45.5 all-gather.4
